TPU v7x, 512 devices: a whole 4x4x16 slice. The times are simulated.
512 devices in a mesh: row: 16 (over z), col: 4 (over x_hi, core), depth: 8 (over y, x_lo).
Axes of the slice: x: 4 (x_hi: 2, x_lo: 2; x = x_hi * 2 + x_lo), y: 4, z: 16, core: 2. Of those that a mesh axis runs over, the one named last changes fastest.
Arguments:
- ks_matrix: bfloat16 [4096, 16384], P('col', ('row', 'depth')), may hold values from -6 to 6
- sign_matrix: bfloat16 [16, 8, 128, 12288], P('col', 'depth', None, 'row'), may hold values from -0.046875 to 0.046875
- ks_mask: int32 [32, 128], P('col', ('row', 'depth')), may hold values 0 or 1
- sign_mask: int32 [16, 8, 1, 96], P('col', 'depth', None, 'row'), may hold values 0 or 1
- product_mask: int32 [32, 96], P('col', 'row'), may hold values 0 or 1
- row_order: int32 [4, 8], P('col'), may hold values from 0 to 7, each once within a row
Outputs:
- next_matrix: bfloat16 [4096, 12288], P(('col', 'depth'), 'row')
Inputs may be any that keep to these rules, and one draw needn't show every extreme that they name: Each row of row_order names every number of 0 to 7 once.
All inputs are finite; a program needn't handle non-finite values. No bound on the sum of `ks_mask` or of `sign_mask` or of `product_mask` on one device may be relied on, other than what follows from the above.
Results may differ from a plain program's by a relative error of at most 0.001.
Values may be sent and summed in bfloat16 or wider, within the bound.
No kernel may reach another device: no remote copies, remote signals or barrier semaphores. Data moves between devices by JAX's collectives and lax.ppermute only.
A program may use at most 64 MiB of HBM per device.

v0:
```python
import jax
import jax.numpy as jnp
from jax import lax
from jax.sharding import PartitionSpec as P

BS = 128


def per_device(ks_matrix, sign_matrix, ks_mask, sign_mask, product_mask, row_order):
    row_blocks, inner_blocks = ks_mask.shape
    local_groups = sign_mask.shape[0]
    sign_inner = sign_mask.shape[2]
    col_blocks = sign_mask.shape[3]
    ks_panel = (
        ks_matrix.reshape(row_blocks, BS, inner_blocks, BS)
        * ks_mask.astype(jnp.bfloat16)[:, None, :, None]
    )
    ks_panel = ks_panel.reshape(row_blocks * BS, inner_blocks * BS)
    sign_kept = sign_matrix.reshape(local_groups, sign_inner, BS, col_blocks, BS)
    sign_kept = sign_kept * sign_mask.astype(jnp.bfloat16).reshape(
        local_groups, sign_inner, 1, col_blocks, 1
    )
    sign_kept = sign_kept.reshape(local_groups, sign_inner * BS, col_blocks * BS)
    sign_whole = lax.all_gather(sign_kept, "col", axis=0, tiled=True)
    ks_whole = lax.all_gather(ks_panel, "row", axis=0, tiled=False)
    product = jnp.einsum("sik,skn->in", ks_whole, sign_whole, preferred_element_type=jnp.float32)
    filtered = (
        product.reshape(row_blocks, BS, col_blocks, BS)
        * product_mask.astype(jnp.float32)[:, None, :, None]
    )
    arranged = jnp.take(filtered, row_order[0], axis=0)
    arranged = arranged.reshape(row_blocks * BS, col_blocks * BS)
    summed = lax.psum_scatter(arranged, "depth", scatter_dimension=0, tiled=True)
    return summed.astype(jnp.bfloat16)


def solution(mesh):
    in_specs = (
        P("col", ("row", "depth")),
        P("col", "depth", None, "row"),
        P("col", ("row", "depth")),
        P("col", "depth", None, "row"),
        P("col", "row"),
        P("col", None),
    )
    out_specs = P(("col", "depth"), "row")
    return jax.shard_map(
        per_device, mesh=mesh, in_specs=in_specs, out_specs=out_specs, check_vma=False
    )
```

profile of v0, /device:TPU:1, one launch (start us, length us, event | category | flops | bytes accessed | tf_op | source)
XLA Modules:
  0.0 242.5 jit_solution(16776493205895536926)
XLA Ops:
  6.5 0.0 copy-start
  6.5 0.0 copy-start.1
  6.5 0.0 all-gather.4.cloned.1.call-start
  6.5 0.7 convert_element_type.13
  7.3 0.1 broadcast_bitcast_fusion
  7.3 2.1 bitcast_multiply_fusion
  9.4 0.0 all-gather.4.cloned.1.call-update
  9.4 0.0 all-gather.6.cloned.1.call-start
  9.5 0.7 convert_bitcast_fusion
  10.2 0.1 broadcast_bitcast_fusion.2
  10.2 1.9 broadcast_multiply_fusion.1
  12.1 0.0 all-gather.6.cloned.1.call-update
  12.2 0.0 reduce-scatter.2.cloned.1.call-start
  12.2 0.0 copy-done
  12.2 0.0 copy-done.1
  12.3 0.1 broadcast_bitcast_fusion.1
  12.4 43.2 %all-gather.4.cloned.1.call-done = bf16[16,128,768]{2,1,0:T(8,128)(2,1)} async-done(((bf16[4,128,768]{2,1,0:T(8,128)(2,1)}), bf16[16,128,768]{2,1,0:T(8,128)(2,1)}) %all-gather.4.cloned.1.call-update) | async-done | bytes 3145744 | tf_op jit(solution)/shard_map/all_gather | solution.py:24
  55.5 71.2 %all-gather.6.cloned.1.call-done = bf16[16384,128]{1,0:T(8,128)(2,1)} async-done(((bf16[1024,128]{1,0:T(8,128)(2,1)}), bf16[16384,128]{1,0:T(8,128)(2,1)}) %all-gather.6.cloned.1.call-update) | async-done | bytes 4194320 | tf_op jit(solution)/shard_map/all_gather | solution.py:25
  126.7 6.2 %convolution_bitcast_fusion = f32[96,8,8,128]{3,1,2,0:T(8,128)S(1)} fusion(bf16[16,1024,128]{2,1,0:T(8,128)(2,1)} %bitcast.42, bf16[16,128,768]{2,1,0:T(8,128)(2,1)} %all-gather.4.cloned.1.call-done), kind=kOutput, calls=%fused_computation.2 | convolution fusion | flops 3221225472 | bytes 10485760 | tf_op jit(solution)/shard_map/sik,skn->in/dot_general | solution.py:26
  132.9 0.7 copy.22
  133.7 2.3 copy.15
  136.0 3.8 %broadcast_multiply_fusion = f32[8,128,6,128]{3,1,2,0:T(8,128)} fusion(f32[8,128,6,128]{3,1,2,0:T(8,128)} %copy.15, f32[8,6]{1,0:T(8,128)S(1)} %convert_element_type.14), kind=kLoop, calls=%fused_computation.3 | loop fusion | flops 786432 | bytes 6291648 | tf_op jit(solution)/shard_map/mul | solution.py:28
  139.8 2.6 %gather_fusion = f32[8,128,6,128]{3,1,2,0:T(8,128)S(1)} fusion(f32[8,128,6,128]{3,1,2,0:T(8,128)} %broadcast_multiply_fusion, s32[1024]{0:T(1024)S(1)} %pad_clamp_fusion), kind=kCustom, calls=%fused_computation | custom fusion | bytes 6291488 | tf_op jit(solution)/shard_map/jit(_take)/gather | solution.py:31
  142.5 2.4 copy.16
  144.9 4.3 %bitcast_select_fusion = f32[1024,768]{0,1:T(8,128)} fusion(f32[96,8,8,128]{3,2,1,0:T(8,128)} %bitcast.39, pred[1024]{0:T(1024)(128)(4,1)S(1)} %broadcast_bitcast_fusion.1), kind=kLoop, calls=%fused_computation.1 | loop fusion | flops 786432 | bytes 6292480 | tf_op jit(solution)/shard_map/jit(_take)/select_n | solution.py:31
  149.2 0.0 reduce-scatter.2.cloned.1.call-update
  149.2 84.9 %reduce-scatter.2.cloned.1.call-done = f32[128,768]{0,1:T(8,128)} async-done(((f32[1024,768]{0,1:T(8,128)}), f32[128,768]{0,1:T(8,128)}) %reduce-scatter.2.cloned.1.call-update) | async-done | bytes 393232 | tf_op jit(solution)/shard_map/reduce_scatter | solution.py:33
  234.1 1.0 convert_element_type.15
  235.1 0.8 copy.17
  (6 shorter events, 0.0 us)
Async XLA Ops:
  6.5 5.7 %copy-start = (s32[8,6]{1,0:T(8,128)S(1)}, s32[8,6]{1,0:T(8,128)}, u32[]{:S(2)}) copy-start(s32[8,6]{1,0:T(8,128)} %param.10) | copy-start | bytes 580
  6.5 5.7 %copy-start.1 = (s32[1,8]{1,0:T(1,128)S(1)}, s32[1,8]{1,0:T(1,128)}, u32[]{:S(2)}) copy-start(s32[1,8]{1,0:T(1,128)} %param.11) | copy-start | bytes 100
  6.5 49.0 %all-gather.4.cloned.1.call-start = ((), (), s32[]{:S(2)}) async-start(), calls=%async_computation.1 | async-start | bytes 3932160 | tf_op jit(solution)/shard_map/all_gather | solution.py:24
  9.4 117.3 %all-gather.6.cloned.1.call-start = ((), (), s32[]{:S(2)}) async-start(), calls=%async_computation.3 | async-start | bytes 4456448 | tf_op jit(solution)/shard_map/all_gather | solution.py:25
  12.2 221.9 %reduce-scatter.2.cloned.1.call-start = ((), (), s32[]{:S(2)}) async-start(), calls=%async_computation.2 | async-start | bytes 3538944 | tf_op jit(solution)/shard_map/reduce_scatter | solution.py:33
Sparse Core Ops, SparseCore 0:
  9.6 45.9 all-gather.3
  57.6 69.0 all-gather.5
  149.3 84.7 reduce-scatter.1
where the time goes:
time: 243 us; the launch traced here: 242 us
  waiting for transfers between devices  199 us (82%)
  other arithmetic  14.5 us (6%)
  between operations  13.2 us (5%)
  local copies, waits for them, and re-layouts  9.19 us (4%)
  matrix products  6.23 us (3%)
    reduce_scatter x1, waiting for transfers between devices, per_device(): lax.psum_scatter(arranged, 'depth', scatter_dimension=0, tiled=True)  84.9 us
    all_gather x1, waiting for transfers between devices, per_device(): ks_whole = lax.all_gather(ks_panel, 'row', axis=0, tiled=False)  71.2 us
    all_gather x1, waiting for transfers between devices, per_device(): sign_whole = lax.all_gather(sign_kept, 'col', axis=0, tiled=True)  43.2 us
    dot_general x1, matrix products, per_device(): jnp.einsum('sik,skn->in', ks_whole, sign_whole, preferred_element_type=jn...  6.23 us
    gather x2, local copies, waits for them, and re-layouts, per_device(): arranged = jnp.take(filtered, row_order[0], axis=0)  5.03 us
  transfers between devices with their start and end apart: 3, of which 3 were waited for; matrix products, arithmetic and copies ran while one was open for 1% of the time, Pallas kernels for 0%

commit v1 on v0

--- a/solution.py
+++ b/solution.py
@@ -21,7 +21,10 @@
         local_groups, sign_inner, 1, col_blocks, 1
     )
     sign_kept = sign_kept.reshape(local_groups, sign_inner * BS, col_blocks * BS)
-    sign_whole = lax.all_gather(sign_kept, "col", axis=0, tiled=True)
+    state_next = lax.axis_size("col")
+    block_now = jnp.stack([sign_kept] * state_next)
+    v1 = lax.all_to_all(block_now, axis_name="col", split_axis=0, concat_axis=0)
+    sign_whole = jnp.concatenate(v1, axis=0)
     ks_whole = lax.all_gather(ks_panel, "row", axis=0, tiled=False)
     product = jnp.einsum("sik,skn->in", ks_whole, sign_whole, preferred_element_type=jnp.float32)
     filtered = (

time: 243 us -> 195 us (0.80)
  waiting for transfers between devices: 199 us -> 142 us
  starting transfers between devices: 0.09 us -> 10.7 us
  other arithmetic: 14.5 us -> 9.76 us
  local copies, waits for them, and re-layouts: 9.19 us -> 11.9 us
    all_gather x1, waiting for transfers between devices: 71.2 us -> 19.7 us  [per_device(): ks_whole = lax.all_gather(ks_panel, 'row', axis=0, tiled=False)]
    all_gather x1 -> x0, waiting for transfers between devices: 43.2 us -> none  [per_device(): sign_whole = lax.all_gather(sign_kept, 'col', axis=0, tiled=True)]
    all_to_all x0 -> x1, waiting for transfers between devices: none -> 37.4 us  [per_device(): v1 = lax.all_to_all(block_now, axis_name='col', split_axis=0, concat_axis=0)]
    all_to_all x0 -> x1, starting transfers between devices: none -> 10.7 us  [per_device(): v1 = lax.all_to_all(block_now, axis_name='col', split_axis=0, concat_axis=0)]
    mul x1 -> x0, other arithmetic: 3.8 us -> none  [per_device(): product.reshape(row_blocks, BS, col_blocks, BS)]
    all_to_all x0 -> x1, local copies, waits for them, and re-layouts: none -> 2.75 us  [per_device(): v1 = lax.all_to_all(block_now, axis_name='col', split_axis=0, concat_axis=0)]
    another operation x0 -> x1, local copies, waits for them, and re-layouts: none -> 2.48 us  [per_device(): block_now = jnp.stack([sign_kept] * state_next)]
  transfers between devices with their start and end apart: 3 -> 3, of which waited for: 3 -> 3; matrix products, arithmetic and copies ran while one was open for 1% -> 4% of each run, Pallas kernels for 0% -> 0%
where the time goes in v1:
time: 195 us
  waiting for transfers between devices  142 us (73%)
  between operations  13.5 us (7%)
  local copies, waits for them, and re-layouts  11.9 us (6%)
  starting transfers between devices  10.7 us (5%)
  other arithmetic  9.76 us (5%)
  matrix products  7.39 us (4%)
    reduce_scatter x1, waiting for transfers between devices, per_device(): lax.psum_scatter(arranged, 'depth', scatter_dimension=0, tiled=True)  84.6 us
    all_to_all x1, waiting for transfers between devices, per_device(): v1 = lax.all_to_all(block_now, axis_name='col', split_axis=0, concat_axis=0)  37.4 us
    all_gather x1, waiting for transfers between devices, per_device(): ks_whole = lax.all_gather(ks_panel, 'row', axis=0, tiled=False)  19.7 us
    all_to_all x1, starting transfers between devices, per_device(): v1 = lax.all_to_all(block_now, axis_name='col', split_axis=0, concat_axis=0)  10.7 us
    dot_general x1, matrix products, per_device(): jnp.einsum('sik,skn->in', ks_whole, sign_whole, preferred_element_type=jn...  7.39 us
    gather x2, local copies, waits for them, and re-layouts, per_device(): arranged = jnp.take(filtered, row_order[0], axis=0)  5.02 us
    select_n x2, other arithmetic, per_device(): arranged = jnp.take(filtered, row_order[0], axis=0)  4.35 us
  transfers between devices with their start and end apart: 3, of which 3 were waited for; matrix products, arithmetic and copies ran while one was open for 4% of the time, Pallas kernels for 0%

profile of v1, /device:TPU:1, one launch (start us, length us, event | category | flops | bytes accessed | tf_op | source)
XLA Modules:
  0.0 195.0 jit_solution(847398949806964526)
XLA Ops:
  6.5 0.0 all-gather.3.cloned.1.call-start
  6.5 0.7 convert_bitcast_fusion
  7.2 0.1 broadcast_bitcast_fusion.2
  7.3 1.8 broadcast_multiply_fusion
  9.1 0.0 all-gather.3.cloned.1.call-update
  9.1 0.7 convert_element_type.13
  9.8 0.1 broadcast_bitcast_fusion
  9.9 1.2 bitcast_multiply_fusion.1
  11.1 0.6 copy.19
  11.7 2.5 %stack.3 = bf16[4,4,128,768]{2,1,3,0:T(4,128)(2,1)} broadcast(bf16[4,128,768]{1,0,2:T(4,128)(2,1)S(1)} %copy.19), dimensions={1,2,3} | broadcast | bytes 3932160 | tf_op jit(solution)/shard_map/stack | solution.py:25
  14.2 0.0 copy-start
  14.2 0.0 copy-start.1
  14.2 10.7 %all-to-all-start = ((bf16[4,4,128,768]{2,1,3,0:T(4,128)(2,1)}), bf16[4,4,128,768]{2,1,3,0:T(4,128)(2,1)S(1)}, u32[]{:S(2)}, u32[]{:S(2)}) async-start(bf16[4,4,128,768]{2,1,3,0:T(4,128)(2,1)} %stack.3), calls=%async_computation | async-start | bytes 6291456 | tf_op jit(solution)/shard_map/all_to_all | solution.py:26
  24.9 0.0 reduce-scatter.2.cloned.1.call-start
  24.9 0.0 copy-done
  24.9 0.0 copy-done.1
  24.9 0.1 broadcast_bitcast_fusion.1
  25.0 37.4 %all-to-all-done = bf16[4,4,128,768]{2,1,3,0:T(4,128)(2,1)S(1)} async-done(((bf16[4,4,128,768]{2,1,3,0:T(4,128)(2,1)}), bf16[4,4,128,768]{2,1,3,0:T(4,128)(2,1)S(1)}, u32[]{:S(2)}, u32[]{:S(2)}) %all-to-all-start) | async-done | bytes 3145760 | tf_op jit(solution)/shard_map/all_to_all | solution.py:26
  62.5 2.8 %copy.20 = bf16[4,4,128,768]{2,1,0,3:T(4,128)(2,1)} copy(bf16[4,4,128,768]{2,1,3,0:T(4,128)(2,1)S(1)} %all-to-all-done) | data formatting | bytes 6291456 | tf_op jit(solution)/shard_map/all_to_all | solution.py:26
  65.2 19.7 %all-gather.3.cloned.1.call-done = bf16[16384,128]{1,0:T(8,128)(2,1)} async-done(((bf16[1024,128]{1,0:T(8,128)(2,1)}), bf16[16384,128]{1,0:T(8,128)(2,1)}) %all-gather.3.cloned.1.call-update) | async-done | bytes 4194320 | tf_op jit(solution)/shard_map/all_gather | solution.py:28
  84.9 7.4 %bitcast_multiply_fusion = f32[8,128,6,128]{3,1,2,0:T(8,128)} fusion(bf16[6,128,128,16]{2,3,1,0:T(8,128)(2,1)} %bitcast.49, bf16[8,128,128,16,1]{2,1,0,3,4:T(8,128)(2,1)} %bitcast.52, f32[8,6]{1,0:T(8,128)S(1)} %convert_element_type.14), kind=kOutput, calls=%fused_computation.4 | convolution fusion | flops 3222011904 | bytes 10485952 | tf_op jit(solution)/shard_map/sik,skn->in/dot_general | solution.py:29
  92.3 2.6 %gather_fusion = f32[8,128,6,128]{3,1,2,0:T(8,128)S(1)} fusion(f32[8,128,6,128]{3,1,2,0:T(8,128)} %bitcast_multiply_fusion, s32[1024]{0:T(1024)S(1)} %pad_clamp_fusion), kind=kCustom, calls=%fused_computation | custom fusion | bytes 6291488 | tf_op jit(solution)/shard_map/jit(_take)/gather | solution.py:34
  95.0 2.4 %copy.23 = f32[8,128,6,128]{1,0,3,2:T(8,128)} copy(f32[8,128,6,128]{3,1,2,0:T(8,128)S(1)} %gather_fusion) | data formatting | bytes 6291456 | tf_op jit(solution)/shard_map/jit(_take)/gather | solution.py:34
  97.4 4.3 %bitcast_select_fusion = f32[1024,768]{0,1:T(8,128)} fusion(f32[96,8,8,128]{3,2,1,0:T(8,128)} %bitcast.48, pred[1024]{0:T(1024)(128)(4,1)S(1)} %broadcast_bitcast_fusion.1), kind=kLoop, calls=%fused_computation.3 | loop fusion | flops 786432 | bytes 6292480 | tf_op jit(solution)/shard_map/jit(_take)/select_n | solution.py:34
  101.7 0.0 reduce-scatter.2.cloned.1.call-update
  101.7 84.6 %reduce-scatter.2.cloned.1.call-done = f32[128,768]{0,1:T(8,128)} async-done(((f32[1024,768]{0,1:T(8,128)}), f32[128,768]{0,1:T(8,128)}) %reduce-scatter.2.cloned.1.call-update) | async-done | bytes 393232 | tf_op jit(solution)/shard_map/reduce_scatter | solution.py:36
  186.3 1.0 convert_element_type.15
  187.4 0.8 copy.24
  (6 shorter events, 0.0 us)
Async XLA Ops:
  6.5 78.4 %all-gather.3.cloned.1.call-start = ((), (), s32[]{:S(2)}) async-start(), calls=%async_computation.3 | async-start | bytes 4456448 | tf_op jit(solution)/shard_map/all_gather | solution.py:28
  14.2 10.7 %copy-start = (s32[8,6]{1,0:T(8,128)S(1)}, s32[8,6]{1,0:T(8,128)}, u32[]{:S(2)}) copy-start(s32[8,6]{1,0:T(8,128)} %param.10) | copy-start | bytes 580
  14.2 10.7 %copy-start.1 = (s32[1,8]{1,0:T(1,128)S(1)}, s32[1,8]{1,0:T(1,128)}, u32[]{:S(2)}) copy-start(s32[1,8]{1,0:T(1,128)} %param.11) | copy-start | bytes 100
  14.2 48.2 %all-to-all-start = ((bf16[4,4,128,768]{2,1,3,0:T(4,128)(2,1)}), bf16[4,4,128,768]{2,1,3,0:T(4,128)(2,1)S(1)}, u32[]{:S(2)}, u32[]{:S(2)}) async-start(bf16[4,4,128,768]{2,1,3,0:T(4,128)(2,1)} %stack.3), calls=%async_computation | async-start | bytes 6291456 | tf_op jit(solution)/shard_map/all_to_all | solution.py:26
  24.9 161.5 %reduce-scatter.2.cloned.1.call-start = ((), (), s32[]{:S(2)}) async-start(), calls=%async_computation.2 | async-start | bytes 3538944 | tf_op jit(solution)/shard_map/reduce_scatter | solution.py:36
Sparse Core Ops, SparseCore 0:
  9.4 75.4 all-gather.2
  101.8 84.4 reduce-scatter.1
